TPU v7x, 512 devices: a whole 4x4x16 slice. The times are simulated.
512 devices in a mesh: lon: 64 (over x, y, z_hi, core), lat: 8 (over z_lo).
Axes of the slice: x: 4, y: 4, z: 16 (z_hi: 2, z_lo: 8; z = z_hi * 8 + z_lo), core: 2. Of those that a mesh axis runs over, the one named last changes fastest.
Arguments:
- potential_heat: float32 [4, 768, 8192], P(None, 'lat', 'lon'), may hold values from -6 to 6
- salt_anomaly_field: float32 [4, 768, 8192], P(None, 'lat', 'lon'), may hold values from -6 to 6
- zonal_current: float32 [4, 768, 8192], P(None, 'lat', 'lon'), may hold values from -6 to 6
- meridional_current: float32 [4, 768, 8192], P(None, 'lat', 'lon'), may hold values from -6 to 6
- water_indicator: int32 [4, 768, 8192], P(None, 'lat', 'lon'), may hold values 0 or 1
- floor_layer_index: int32 [768, 8192], P('lat', 'lon'), may hold values from 0 to 3
- zonal_spacing: float32 [768, 8192], P('lat', 'lon'), may hold values from 0.7 to 1.4
- meridional_spacing: float32 [768, 8192], P('lat', 'lon'), may hold values from 0.7 to 1.4
- planetary_rotation_factor: float32 [768, 8192], P('lat', 'lon'), may hold values from 0.3 to 1.5
- horizontal_eddy_coefficient: float32 [768, 8192], P('lat', 'lon'), may hold values from 0.05 to 0.25
- diapycnal_diffusivity: float32 [3, 768, 8192], P(None, 'lat', 'lon'), may hold values from 0.02 to 0.5
- layer_height: float32 [4], replicated, may hold values from 0.7 to 1.4
Outputs:
- new_temperature: float32 [4, 768, 8192], P(None, 'lat', 'lon')
- new_salinity: float32 [4, 768, 8192], P(None, 'lat', 'lon')
- new_zonal: float32 [4, 768, 8192], P(None, 'lat', 'lon')
- new_meridional: float32 [4, 768, 8192], P(None, 'lat', 'lon')
All inputs are finite; a program needn't handle non-finite values. No bound on the sum of `water_indicator` on one device may be relied on, other than what follows from the above.
Results may differ from a plain program's by a relative error of at most 0.0003.
Values sent between devices are 32-bit elements; how exact they have to be, the bound alone decides.
No kernel may reach another device: no remote copies, remote signals or barrier semaphores. Data moves between devices by JAX's collectives and lax.ppermute only.
A program may use at most 64 MiB of HBM per device.

v0:
```python
import jax
import jax.numpy as jnp
from jax import lax
from jax.sharding import PartitionSpec as P

TIME_STEP = 0.25
EXPANSION = 0.2
CONTRACTION = 0.8
BOTTOM_DRAG = 1.0


def with_halo(value, sides, width, wrap):
    for axis, dim in sides:
        size, length = (lax.axis_size(axis), value.shape[dim])
        up = [(i, (i + 1) % size) for i in range(size if wrap else size - 1)]
        down = [(j, i) for i, j in up]
        last = lax.slice_in_dim(value, length - width, length, axis=dim)
        leading = lax.slice_in_dim(value, 0, width, axis=dim)
        before = lax.ppermute(last, axis, up)
        after = lax.ppermute(leading, axis, down)
        value = jnp.concatenate([before, value, after], axis=dim)
    return value


def pressure(temp_part, salt_part, layer_height):
    layer_mass = (CONTRACTION * salt_part - EXPANSION * temp_part) * layer_height[:, None, None]
    return jnp.cumsum(layer_mass, axis=0) - 0.5 * layer_mass


def mix_vertically(fields, water_share, diapycnal_diffusivity, layer_height):
    contrast = fields[:, 1:] - fields[:, :-1]
    fluxes = diapycnal_diffusivity * (water_share[1:] * water_share[:-1]) * contrast
    boundary = jnp.zeros_like(fluxes[:, :1])
    flux_below = jnp.concatenate([fluxes, boundary], axis=1)
    flux_above = jnp.concatenate([boundary, fluxes], axis=1)
    return (flux_below - flux_above) / (layer_height * layer_height)[None, :, None, None]


def advance(
    central,
    eastern,
    western,
    northern,
    southern,
    at_bottom,
    zonal_spacing,
    meridional_spacing,
    planetary_rotation_factor,
    horizontal_eddy_coefficient,
    diapycnal_diffusivity,
    layer_height,
):
    water_share = central[4]
    fields = central[:4]
    weight_east = water_share * eastern[4]
    weight_west = water_share * western[4]
    weight_north = water_share * northern[4]
    weight_south = water_share * southern[4]
    diffusion = horizontal_eddy_coefficient * (
        (weight_east * (eastern[:4] - fields) + weight_west * (western[:4] - fields))
        / (zonal_spacing * zonal_spacing)
        + (weight_north * (northern[:4] - fields) + weight_south * (southern[:4] - fields))
        / (meridional_spacing * meridional_spacing)
    )
    zonal = fields[2]
    merid = fields[3]
    advection = -(
        zonal * (eastern[:4] - western[:4]) * (0.5 / zonal_spacing)
        + merid * (northern[:4] - southern[:4]) * (0.5 / meridional_spacing)
    )
    pressure_east = pressure(eastern[0], eastern[1], layer_height)
    pressure_west = pressure(western[0], western[1], layer_height)
    pressure_north = pressure(northern[0], northern[1], layer_height)
    pressure_south = pressure(southern[0], southern[1], layer_height)
    gradient_x = -(pressure_east - pressure_west) * (0.5 / zonal_spacing)
    gradient_y = -(pressure_north - pressure_south) * (0.5 / meridional_spacing)
    mixing = mix_vertically(fields, water_share, diapycnal_diffusivity, layer_height)
    tendency = advection + diffusion + mixing
    tend_zonal = (
        tendency[2]
        + planetary_rotation_factor * merid
        + gradient_x
        - BOTTOM_DRAG * at_bottom * zonal
    )
    tend_merid = (
        tendency[3]
        - planetary_rotation_factor * zonal
        + gradient_y
        - BOTTOM_DRAG * at_bottom * merid
    )
    tendency = jnp.stack([tendency[0], tendency[1], tend_zonal, tend_merid])
    updated = water_share * (fields + TIME_STEP * tendency)
    return jnp.concatenate([updated, water_share[None]], axis=0)


def fold_ghost(top_row):
    fold_sign = jnp.array([1.0, 1.0, -1.0, -1.0, 1.0], jnp.float32).reshape(5, 1, 1)
    row_width = top_row.shape[2]
    gathered = lax.all_gather(top_row, "lon", axis=2, tiled=True)
    partner = lax.axis_size("lon") - 1 - lax.axis_index("lon")
    mirrored = lax.dynamic_slice_in_dim(gathered, partner * row_width, row_width, 2)
    return mirrored[:, :, ::-1] * fold_sign


def shards(
    potential_heat,
    salt_anomaly_field,
    zonal_current,
    meridional_current,
    water_indicator,
    floor_layer_index,
    zonal_spacing,
    meridional_spacing,
    planetary_rotation_factor,
    horizontal_eddy_coefficient,
    diapycnal_diffusivity,
    layer_height,
):
    water_share = water_indicator.astype(jnp.float32)
    combined_tracers = jnp.stack(
        [
            potential_heat * water_share,
            salt_anomaly_field * water_share,
            zonal_current * water_share,
            meridional_current * water_share,
            water_share,
        ]
    )
    levels = combined_tracers.shape[1]
    is_top = lax.axis_index("lat") == lax.axis_size("lat") - 1
    at_bottom = (
        lax.broadcasted_iota(jnp.int32, (levels, 1, 1), 0) == floor_layer_index[None]
    ).astype(jnp.float32)
    for step_index in range(2):
        lon_padded = with_halo(combined_tracers, (("lon", 3),), 1, True)
        lat_padded = with_halo(combined_tracers, (("lat", 2),), 1, False)
        ghost_row = fold_ghost(combined_tracers[:, :, -1, :])
        north_rim = jnp.where(is_top, ghost_row, lat_padded[:, :, -1, :])
        northern = jnp.concatenate([lat_padded[:, :, 2:-1, :], north_rim[:, :, None, :]], axis=2)
        southern = lat_padded[:, :, :-2, :]
        eastern = lon_padded[..., 2:]
        western = lon_padded[..., :-2]
        combined_tracers = advance(
            combined_tracers,
            eastern,
            western,
            northern,
            southern,
            at_bottom,
            zonal_spacing,
            meridional_spacing,
            planetary_rotation_factor,
            horizontal_eddy_coefficient,
            diapycnal_diffusivity,
            layer_height,
        )
    return (combined_tracers[0], combined_tracers[1], combined_tracers[2], combined_tracers[3])


def solution(mesh):
    return jax.shard_map(
        shards,
        mesh=mesh,
        in_specs=(
            P(None, "lat", "lon"),
            P(None, "lat", "lon"),
            P(None, "lat", "lon"),
            P(None, "lat", "lon"),
            P(None, "lat", "lon"),
            P("lat", "lon"),
            P("lat", "lon"),
            P("lat", "lon"),
            P("lat", "lon"),
            P("lat", "lon"),
            P(None, "lat", "lon"),
            P(),
        ),
        out_specs=(
            P(None, "lat", "lon"),
            P(None, "lat", "lon"),
            P(None, "lat", "lon"),
            P(None, "lat", "lon"),
        ),
        check_vma=False,
    )
```

profile of v0, /device:TPU:96, one launch (start us, length us, event | category | flops | bytes accessed | tf_op | source)
XLA Modules:
  0.0 402.4 jit_solution(17297029420401216242)
XLA Ops:
  0.7 1.1 constant_dynamic-update-slice_fusion.4
  1.8 1.1 constant_dynamic-update-slice_fusion.3
  2.9 1.1 constant_dynamic-update-slice_fusion.2
  4.1 0.6 fusion.150
  4.7 2.0 collective-permute-start.2
  6.8 5.0 %collective-permute-start.3 = (f32[5,4,1,128]{3,2,1,0:T(1,128)}, f32[5,4,1,128]{3,2,1,0:T(1,128)S(1)}, u32[]{:S(2)}, u32[]{:S(2)}) collective-permute-start(f32[5,4,1,128]{3,2,1,0:T(1,128)} %get-tuple-element.27), channel_id=1, source_target_pairs={{0,1},{1,2},{2,3},{3,4},{4,5},{5,6},{6,7},{8,9},{9,10},{10,11},{11... | collective-permute-start | bytes 30728 | tf_op jit(solution)/shard_map/ppermute | solution.py:19
  11.8 1.3 fusion.149
  13.1 2.2 copy.83
  15.2 16.5 %collective-permute-start = (f32[5,4,96,1]{2,1,3,0:T(4,128)}, f32[5,4,96,1]{2,1,3,0:T(4,128)}, u32[]{:S(2)}, u32[]{:S(2)}) collective-permute-start(f32[5,4,96,1]{2,1,3,0:T(4,128)} %copy.83), channel_id=1, source_target_pairs={{8,0},{16,8},{24,16},{32,24},{40,32},{48,40},{56,48},{64,56},{72,6... | collective-permute-start | bytes 23048 | tf_op jit(solution)/shard_map/ppermute | solution.py:20
  31.8 0.3 copy.85
  32.1 1.9 collective-permute-start.1
  34.1 150.4 %all-gather = f32[5,4,1,8192]{3,2,1,0:T(1,128)S(1)} all-gather(f32[5,4,1,128]{3,2,1,0:T(1,128)} %get-tuple-element.27), channel_id=2, replica_groups=mesh['lon'=64,'lat'=8] {'lon'}, dimensions={3}, use_global_device_ids=true | all-gather | bytes 665600 | tf_op jit(solution)/shard_map/all_gather | solution.py:99
  184.7 0.9 fusion.35
  185.6 0.7 broadcast_divide_fusion
  186.4 0.7 rev.6
  187.1 0.5 mul.524
  187.7 1.1 copy.86
  188.7 1.0 reduce-window_subtract_fusion.6
  189.7 2.0 copy.84
  191.7 0.8 bitcast_select_fusion
  192.6 1.4 fusion.74
  194.3 1.3 divide_add_fusion.1
  195.7 0.5 fusion.20
  196.5 0.4 copy-done.15
  196.9 0.4 copy-done.13
  197.4 1.3 fusion.22
  198.8 164.6 %all-gather.1 = f32[5,4,1,8192]{3,2,1,0:T(1,128)} all-gather(f32[5,4,1,128]{3,2,1,0:T(1,128)S(1)} %get-tuple-element.23), channel_id=3, replica_groups=mesh['lon'=64,'lat'=8] {'lon'}, dimensions={3}, use_global_device_ids=true | all-gather | bytes 665600 | tf_op jit(solution)/shard_map/all_gather | solution.py:99
  363.4 1.9 collective-permute-start.7
  365.3 0.9 fusion.34
  366.2 0.8 slice_bitcast_fusion.7
  366.9 1.5 copy.91
  368.5 2.3 collective-permute-start.5
  370.7 0.3 copy.89
  371.1 16.2 %collective-permute-start.4 = (f32[5,4,96,1]{2,1,3,0:T(4,128)S(1)}, f32[5,4,96,1]{2,1,3,0:T(4,128)S(1)}, u32[]{:S(2)}, u32[]{:S(2)}) collective-permute-start(f32[5,4,96,1]{2,1,3,0:T(4,128)S(1)} %copy.89), channel_id=1, source_target_pairs={{8,0},{16,8},{24,16},{32,24},{40,32},{48,40},{56,48},{64,56},{72,6... | collective-permute-start | bytes 23048 | tf_op jit(solution)/shard_map/ppermute | solution.py:20
  387.3 0.7 constant_dynamic-slice_fusion
  388.1 3.9 collective-permute-start.6
  392.1 0.4 copy.92
  392.4 1.0 reduce-window_subtract_fusion.2
  393.4 1.3 copy.90
  394.7 1.9 pad_maximum_fusion
  396.8 1.0 copy-done.1
  398.0 0.2 fusion.84
  398.2 0.6 copy-done.6
  399.2 0.2 copy-done.20
  399.6 0.9 divide_add_fusion
  400.5 0.5 fusion.17
  401.3 0.2 fusion.33
  401.5 0.9 slice_bitcast_fusion
  (120 shorter events, 2.3 us)
Async XLA Ops:
  0.6 3.4 copy-start.2
  0.6 3.4 copy-start.41
  1.8 182.9 %copy-start.4 = (f32[1,4,96,128]{3,2,1,0:T(8,128)}, f32[1,4,96,128]{3,2,1,0:T(8,128)S(1)}, u32[]{:S(2)}) copy-start(f32[1,4,96,128]{3,2,1,0:T(8,128)S(1)} %get-tuple-element.11) | copy-start | bytes 589828
  2.9 181.7 %copy-start.7 = (f32[1,4,96,128]{3,2,1,0:T(8,128)}, f32[1,4,96,128]{3,2,1,0:T(8,128)S(1)}, u32[]{:S(2)}) copy-start(f32[1,4,96,128]{3,2,1,0:T(8,128)S(1)} %get-tuple-element.9) | copy-start | bytes 589828
  4.7 187.0 %collective-permute-start.2 = (f32[5,4,1,128]{3,1,0,2:T(4,128)}, f32[5,4,1,128]{3,1,0,2:T(4,128)}, u32[]{:S(2)}, u32[]{:S(2)}) collective-permute-start(f32[5,4,1,128]{3,1,0,2:T(4,128)} %bitcast.37), channel_id=1, source_target_pairs={{1,0},{2,1},{3,2},{4,3},{5,4},{6,5},{7,6},{9,8},{10,9},{11,10},{12... | collective-permute-start | bytes 30728 | tf_op jit(solution)/shard_map/ppermute | solution.py:20
  6.8 185.8 %collective-permute-start.3 = (f32[5,4,1,128]{3,2,1,0:T(1,128)}, f32[5,4,1,128]{3,2,1,0:T(1,128)S(1)}, u32[]{:S(2)}, u32[]{:S(2)}) collective-permute-start(f32[5,4,1,128]{3,2,1,0:T(1,128)} %get-tuple-element.27), channel_id=1, source_target_pairs={{0,1},{1,2},{2,3},{3,4},{4,5},{5,6},{6,7},{8,9},{9,10},{10,11},{11... | collective-permute-start | bytes 30728 | tf_op jit(solution)/shard_map/ppermute | solution.py:19
  13.1 171.5 %copy-start.42 = (f32[3,96,128]{2,1,0:T(8,128)S(1)}, f32[3,96,128]{2,1,0:T(8,128)}, u32[]{:S(2)}) copy-start(f32[3,96,128]{2,1,0:T(8,128)} %param.24) | copy-start | bytes 442372
  15.2 174.5 %collective-permute-start = (f32[5,4,96,1]{2,1,3,0:T(4,128)}, f32[5,4,96,1]{2,1,3,0:T(4,128)}, u32[]{:S(2)}, u32[]{:S(2)}) collective-permute-start(f32[5,4,96,1]{2,1,3,0:T(4,128)} %copy.83), channel_id=1, source_target_pairs={{8,0},{16,8},{24,16},{32,24},{40,32},{48,40},{56,48},{64,56},{72,6... | collective-permute-start | bytes 23048 | tf_op jit(solution)/shard_map/ppermute | solution.py:20
  32.1 155.5 %collective-permute-start.1 = (f32[5,4,96,1]{2,1,3,0:T(4,128)S(1)}, f32[5,4,96,1]{2,1,3,0:T(4,128)}, u32[]{:S(2)}, u32[]{:S(2)}) collective-permute-start(f32[5,4,96,1]{2,1,3,0:T(4,128)S(1)} %copy.85), channel_id=1, source_target_pairs={{0,8},{8,16},{16,24},{24,32},{32,40},{40,48},{48,56},{56,64},{64,7... | collective-permute-start | bytes 23048 | tf_op jit(solution)/shard_map/ppermute | solution.py:19
  184.5 1.1 copy-start.12
  184.6 1.1 copy-start.44
  184.6 1.7 copy-start.21
  184.7 2.4 copy-start.43
  192.5 1.5 copy-start
  192.5 1.5 copy-start.5
  192.6 1.5 copy-start.8
  192.6 1.6 copy-start.19
  192.6 1.6 copy-start.23
  192.6 1.6 copy-start.25
  192.6 1.6 copy-start.35
  192.6 1.6 copy-start.37
  192.6 1.6 copy-start.39
  192.6 1.6 copy-start.47
  194.2 1.4 copy-start.28
  194.3 1.4 copy-start.29
  194.3 1.4 copy-start.31
  197.2 1.4 copy-start.17
  198.7 166.6 %copy-start.22 = (f32[3,96,128]{2,1,0:T(8,128)S(1)}, f32[3,96,128]{2,1,0:T(8,128)}, u32[]{:S(2)}) copy-start(f32[3,96,128]{2,1,0:T(8,128)} %copy-done.21) | copy-start | bytes 442372
  363.4 33.4 %collective-permute-start.7 = (f32[5,4,1,128]{3,2,1,0:T(1,128)S(1)}, f32[5,4,1,128]{3,2,1,0:T(1,128)S(1)}, u32[]{:S(2)}, u32[]{:S(2)}) collective-permute-start(f32[5,4,1,128]{3,2,1,0:T(1,128)S(1)} %get-tuple-element.23), channel_id=1, source_target_pairs={{0,1},{1,2},{2,3},{3,4},{4,5},{5,6},{6,7},{8,9},{9,10},{10,11},{11... | collective-permute-start | bytes 30728 | tf_op jit(solution)/shard_map/ppermute | solution.py:19
  368.5 23.6 %collective-permute-start.5 = (f32[5,4,96,1]{2,1,3,0:T(4,128)S(1)}, f32[5,4,96,1]{2,1,3,0:T(4,128)S(1)}, u32[]{:S(2)}, u32[]{:S(2)}) collective-permute-start(f32[5,4,96,1]{2,1,3,0:T(4,128)S(1)} %copy.91), channel_id=1, source_target_pairs={{0,8},{8,16},{16,24},{24,32},{32,40},{40,48},{48,56},{56,64},{64,7... | collective-permute-start | bytes 23048 | tf_op jit(solution)/shard_map/ppermute | solution.py:19
  371.1 22.3 %collective-permute-start.4 = (f32[5,4,96,1]{2,1,3,0:T(4,128)S(1)}, f32[5,4,96,1]{2,1,3,0:T(4,128)S(1)}, u32[]{:S(2)}, u32[]{:S(2)}) collective-permute-start(f32[5,4,96,1]{2,1,3,0:T(4,128)S(1)} %copy.89), channel_id=1, source_target_pairs={{8,0},{16,8},{24,16},{32,24},{40,32},{48,40},{56,48},{64,56},{72,6... | collective-permute-start | bytes 23048 | tf_op jit(solution)/shard_map/ppermute | solution.py:20
  388.1 8.5 %collective-permute-start.6 = (f32[5,4,1,128]{3,2,1,0:T(1,128)S(1)}, f32[5,4,1,128]{3,2,1,0:T(1,128)S(1)}, u32[]{:S(2)}, u32[]{:S(2)}) collective-permute-start(f32[5,4,1,128]{3,2,1,0:T(1,128)S(1)} %get-tuple-element.22), channel_id=1, source_target_pairs={{1,0},{2,1},{3,2},{4,3},{5,4},{6,5},{7,6},{9,8},{10,9},{11,10},{12... | collective-permute-start | bytes 30728 | tf_op jit(solution)/shard_map/ppermute | solution.py:20
  394.7 1.9 copy-start.46
  396.6 1.2 copy-start.1
  396.6 1.2 copy-start.3
  397.8 1.2 copy-start.11
  397.8 1.2 copy-start.14
  397.9 1.3 copy-start.16
  397.9 1.3 copy-start.18
  397.9 1.5 copy-start.20
  397.9 1.5 copy-start.24
  397.9 1.5 copy-start.26
  397.9 1.6 copy-start.33
  397.9 1.6 copy-start.34
  397.9 1.6 copy-start.36
  397.9 1.6 copy-start.38
  397.9 1.6 copy-start.40
  398.0 1.6 copy-start.48
  (9 other events, 8.2 us)
where the time goes:
time: 403 us; the launch traced here: 402 us
  blocking collectives  315 us (78%)
  starting transfers between devices  49.8 us (12%)
  other arithmetic  18.4 us (5%)
  local copies, waits for them, and re-layouts  17.8 us (4%)
    all_gather x2, blocking collectives, fold_ghost(): gathered = lax.all_gather(top_row, 'lon', axis=2, tiled=True)  315 us
    ppermute x4, starting transfers between devices, with_halo(): after = lax.ppermute(leading, axis, down)  38.7 us
    ppermute x4, starting transfers between devices, with_halo(): before = lax.ppermute(last, axis, up)  11.1 us
  transfers between devices with their start and end apart: 8, of which 0 were waited for; matrix products, arithmetic and copies ran while one was open for 5% of the time, Pallas kernels for 0%

commit v1 on v0

--- a/solution.py
+++ b/solution.py
@@ -96,7 +96,9 @@
 def fold_ghost(top_row):
     fold_sign = jnp.array([1.0, 1.0, -1.0, -1.0, 1.0], jnp.float32).reshape(5, 1, 1)
     row_width = top_row.shape[2]
-    gathered = lax.all_gather(top_row, "lon", axis=2, tiled=True)
+    gathered = jnp.concatenate(
+        lax.all_to_all(jnp.stack([top_row] * lax.axis_size("lon")), "lon", 0, 0), axis=2
+    )
     partner = lax.axis_size("lon") - 1 - lax.axis_index("lon")
     mirrored = lax.dynamic_slice_in_dim(gathered, partner * row_width, row_width, 2)
     return mirrored[:, :, ::-1] * fold_sign

time: 403 us -> 154 us (0.38)
  the two profiles are of different devices: /device:TPU:96 before, /device:TPU:32 now
where the time goes in v1:
time: 154 us; the launch traced here: 153 us
  starting transfers between devices  74.4 us (48%)
  waiting for transfers between devices  26.9 us (17%)
  local copies, waits for them, and re-layouts  25.6 us (17%)
  other arithmetic  24.7 us (16%)
    ppermute x4, starting transfers between devices, with_halo(): after = lax.ppermute(leading, axis, down)  38.9 us
    ppermute x4, waiting for transfers between devices, with_halo(): before = lax.ppermute(last, axis, up)  26.9 us
    all_to_all x2, starting transfers between devices, fold_ghost(): lax.all_to_all(jnp.stack([top_row] * lax.axis_size('lon')), 'lon', 0, 0)  26 us
    ppermute x4, starting transfers between devices, with_halo(): before = lax.ppermute(last, axis, up)  9.51 us
    another operation x8, other arithmetic, pressure(): return jnp.cumsum(layer_mass, axis=0) - 0.5 * layer_mass  4.84 us
    unnamed x104, local copies, waits for them, and re-layouts  4.25 us
    ppermute x2, local copies, waits for them, and re-layouts, with_halo(): after = lax.ppermute(leading, axis, down)  4.08 us
    add x2, other arithmetic, advance(): tendency = advection + diffusion + mixing  3.98 us
  transfers between devices with their start and end apart: 10, of which 2 were waited for; matrix products, arithmetic and copies ran while one was open for 18% of the time, Pallas kernels for 0%

profile of v1, /device:TPU:32, one launch (start us, length us, event | category | flops | bytes accessed | tf_op | source)
XLA Modules:
  0.0 153.0 jit_solution(6646809257808822381)
XLA Ops:
  0.7 1.1 constant_dynamic-update-slice_fusion.4
  1.8 1.1 constant_dynamic-update-slice_fusion.3
  2.9 1.1 constant_dynamic-update-slice_fusion.2
  4.1 0.6 fusion.150
  4.7 1.6 %stack.49 = f32[64,5,4,128]{3,2,1,0:T(4,128)} broadcast(f32[5,4,128]{2,1,0:T(4,128)} %bitcast.5), dimensions={1,2,3} | broadcast | bytes 665600 | tf_op jit(solution)/shard_map/stack | solution.py:100
  6.4 20.5 %all-to-all-start = ((f32[64,5,4,128]{3,2,1,0:T(4,128)}), f32[64,5,4,128]{3,2,1,0:T(4,128)}, u32[]{:S(2)}, u32[]{:S(2)}) async-start(f32[64,5,4,128]{3,2,1,0:T(4,128)} %stack.49), calls=%async_computation | async-start | bytes 1310720 | tf_op jit(solution)/shard_map/all_to_all | solution.py:100
  26.9 2.9 %collective-permute-start.3 = (f32[5,4,1,128]{3,2,1,0:T(1,128)}, f32[5,4,1,128]{3,2,1,0:T(1,128)S(1)}, u32[]{:S(2)}, u32[]{:S(2)}) collective-permute-start(f32[5,4,1,128]{3,2,1,0:T(1,128)} %get-tuple-element.27), channel_id=1, source_target_pairs={{0,1},{1,2},{2,3},{3,4},{4,5},{5,6},{6,7},{8,9},{9,10},{10,11},{11... | collective-permute-start | bytes 30728 | tf_op jit(solution)/shard_map/ppermute | solution.py:19
  29.8 2.9 %collective-permute-start.2 = (f32[5,4,1,128]{3,1,0,2:T(4,128)}, f32[5,4,1,128]{3,1,0,2:T(4,128)}, u32[]{:S(2)}, u32[]{:S(2)}) collective-permute-start(f32[5,4,1,128]{3,1,0,2:T(4,128)} %bitcast.39), channel_id=1, source_target_pairs={{1,0},{2,1},{3,2},{4,3},{5,4},{6,5},{7,6},{9,8},{10,9},{11,10},{12... | collective-permute-start | bytes 30728 | tf_op jit(solution)/shard_map/ppermute | solution.py:20
  32.8 1.3 fusion.149
  34.1 2.2 %copy.83 = f32[5,4,96,1]{2,1,3,0:T(4,128)} copy(f32[5,4,96,1]{3,2,1,0:T(8,128)} %get-tuple-element.25) | data formatting | bytes 15360 | tf_op jit(solution)/shard_map/slice | solution.py:18
  36.2 15.8 %collective-permute-start = (f32[5,4,96,1]{2,1,3,0:T(4,128)}, f32[5,4,96,1]{2,1,3,0:T(4,128)}, u32[]{:S(2)}, u32[]{:S(2)}) collective-permute-start(f32[5,4,96,1]{2,1,3,0:T(4,128)} %copy.83), channel_id=1, source_target_pairs={{8,0},{16,8},{24,16},{32,24},{40,32},{48,40},{56,48},{64,56},{72,6... | collective-permute-start | bytes 23048 | tf_op jit(solution)/shard_map/ppermute | solution.py:20
  52.4 1.9 %collective-permute-start.1 = (f32[5,4,96,1]{2,1,3,0:T(4,128)S(1)}, f32[5,4,96,1]{2,1,3,0:T(4,128)}, u32[]{:S(2)}, u32[]{:S(2)}) collective-permute-start(f32[5,4,96,1]{2,1,3,0:T(4,128)S(1)} %copy.85), channel_id=1, source_target_pairs={{0,8},{8,16},{16,24},{24,32},{32,40},{40,48},{48,56},{56,64},{64,7... | collective-permute-start | bytes 23048 | tf_op jit(solution)/shard_map/ppermute | solution.py:19
  54.5 0.7 copy-done.13
  55.2 0.9 fusion.35
  56.1 0.7 broadcast_divide_fusion
  57.4 13.2 %collective-permute-done.1 = f32[5,4,96,1]{2,1,3,0:T(4,128)} collective-permute-done((f32[5,4,96,1]{2,1,3,0:T(4,128)S(1)}, f32[5,4,96,1]{2,1,3,0:T(4,128)}, u32[]{:S(2)}, u32[]{:S(2)}) %collective-permute-start.1) | collective-permute-done | bytes 7712 | tf_op jit(solution)/shard_map/ppermute | solution.py:19
  70.6 1.1 copy.86
  71.7 1.0 reduce-window_subtract_fusion.6
  72.7 2.0 %copy.84 = f32[5,4,96,1]{3,2,1,0:T(8,128)} copy(f32[5,4,96,1]{2,1,3,0:T(4,128)} %collective-permute-done) | data formatting | bytes 15360 | tf_op jit(solution)/shard_map/ppermute | solution.py:20
  74.7 0.8 reduce-window_subtract_fusion.4
  75.5 1.2 copy_bitcast_fusion.1
  77.3 1.4 rev.6
  78.7 0.8 bitcast_select_fusion
  79.6 1.4 fusion.74
  81.2 1.3 divide_add_fusion.1
  83.9 0.8 copy-done.14
  85.4 0.6 pad_maximum_fusion.7
  86.0 0.9 stack.53
  86.9 5.5 %all-to-all-start.1 = ((f32[64,5,4,128]{3,2,1,0:T(4,128)}), f32[64,5,4,128]{3,2,1,0:T(4,128)}, u32[]{:S(2)}, u32[]{:S(2)}) async-start(f32[64,5,4,128]{3,2,1,0:T(4,128)} %stack.53), calls=%async_computation.1 | async-start | bytes 1310720 | tf_op jit(solution)/shard_map/all_to_all | solution.py:100
  92.4 2.7 %collective-permute-start.7 = (f32[5,4,1,128]{3,2,1,0:T(1,128)S(1)}, f32[5,4,1,128]{3,2,1,0:T(1,128)S(1)}, u32[]{:S(2)}, u32[]{:S(2)}) collective-permute-start(f32[5,4,1,128]{3,2,1,0:T(1,128)S(1)} %get-tuple-element.23), channel_id=1, source_target_pairs={{0,1},{1,2},{2,3},{3,4},{4,5},{5,6},{6,7},{8,9},{9,10},{10,11},{11... | collective-permute-start | bytes 30728 | tf_op jit(solution)/shard_map/ppermute | solution.py:19
  95.8 1.9 %collective-permute-start.5 = (f32[5,4,96,1]{2,1,3,0:T(4,128)S(1)}, f32[5,4,96,1]{2,1,3,0:T(4,128)S(1)}, u32[]{:S(2)}, u32[]{:S(2)}) collective-permute-start(f32[5,4,96,1]{2,1,3,0:T(4,128)S(1)} %copy.92), channel_id=1, source_target_pairs={{0,8},{8,16},{16,24},{24,32},{32,40},{40,48},{48,56},{56,64},{64,7... | collective-permute-start | bytes 23048 | tf_op jit(solution)/shard_map/ppermute | solution.py:19
  98.1 16.6 %collective-permute-start.4 = (f32[5,4,96,1]{2,1,3,0:T(4,128)S(1)}, f32[5,4,96,1]{2,1,3,0:T(4,128)}, u32[]{:S(2)}, u32[]{:S(2)}) collective-permute-start(f32[5,4,96,1]{2,1,3,0:T(4,128)S(1)} %copy.90), channel_id=1, source_target_pairs={{8,0},{16,8},{24,16},{32,24},{40,32},{48,40},{56,48},{64,56},{72,6... | collective-permute-start | bytes 23048 | tf_op jit(solution)/shard_map/ppermute | solution.py:20
  114.7 0.8 slice_bitcast_fusion.7
  115.5 0.9 fusion.34
  116.5 3.6 %collective-permute-start.6 = (f32[5,4,1,128]{3,2,1,0:T(1,128)}, f32[5,4,1,128]{3,2,1,0:T(1,128)}, u32[]{:S(2)}, u32[]{:S(2)}) collective-permute-start(f32[5,4,1,128]{3,2,1,0:T(1,128)} %get-tuple-element.22), channel_id=1, source_target_pairs={{1,0},{2,1},{3,2},{4,3},{5,4},{6,5},{7,6},{9,8},{10,9},{11,10},{12... | collective-permute-start | bytes 30728 | tf_op jit(solution)/shard_map/ppermute | solution.py:20
  120.0 13.7 %collective-permute-done.5 = f32[5,4,96,1]{2,1,3,0:T(4,128)S(1)} collective-permute-done((f32[5,4,96,1]{2,1,3,0:T(4,128)S(1)}, f32[5,4,96,1]{2,1,3,0:T(4,128)S(1)}, u32[]{:S(2)}, u32[]{:S(2)}) %collective-permute-start.5) | collective-permute-done | bytes 7712 | tf_op jit(solution)/shard_map/ppermute | solution.py:19
  134.1 2.0 %copy.91 = f32[5,4,96,1]{3,2,1,0:T(8,128)} copy(f32[5,4,96,1]{2,1,3,0:T(4,128)} %collective-permute-done.4) | data formatting | bytes 15360 | tf_op jit(solution)/shard_map/ppermute | solution.py:20
  136.2 1.0 reduce-window_subtract_fusion.2
  137.3 2.6 %pad_maximum_fusion = (f32[5,4,96,129]{3,2,1,0:T(8,128)}, f32[5,4,96,129]{3,2,1,0:T(8,128)}) fusion(f32[5,4,96,1]{3,2,1,0:T(8,128)S(1)} %copy-done.1, f32[1,4,96,128]{3,2,1,0:T(8,128)S(1)} %get-tuple-element.35, f32[4,4,96,128]{3,2,1,0:T(8,128)S(1)} %fusion.31, f32[5,4,96,1]{3,2,1,0:T(8,128)S(1)} %copy.93), kind=kLoop, calls=%fused_computation.19 | loop fusion | flops 990720 | bytes 2979840 | tf_op jit(solution)/shard_map/concatenate | solution.py:21
  140.0 1.1 maximum_maximum_fusion.1
  141.1 0.8 reduce-window_subtract_fusion
  141.9 1.2 copy_bitcast_fusion
  143.1 0.6 constant_dynamic-slice_fusion
  143.7 1.4 rev.7
  145.1 0.8 multiply_select_fusion
  146.1 1.3 fusion.84
  148.1 2.6 %divide_add_fusion = f32[4,4,96,128]{3,2,1,0:T(8,128)S(1)} fusion(f32[4,3,96,128]{3,2,1,0:T(8,128)S(1)} %copy-done.22, f32[5,4,1,128]{3,2,1,0:T(1,128)S(1)} %bitcast.140, f32[5,4,95,128]{3,2,1,0:T(8,128)S(1)} %fusion.24, f32[5,4,97,128]{3,2,1,0:T(8,128)S(1)} %copy-done.16, f32[5,4,96,129]{3,2,1,0:T(8,128)} %get-tuple-element.19, ...), kind=kLoop, calls=%fused_computation.86 | loop fusion | flops 6881280 | bytes 7913488 | tf_op jit(solution)/shard_map/add | solution.py:78
  152.2 0.9 slice_bitcast_fusion
  (132 shorter events, 7.6 us)
Async XLA Ops:
  0.6 3.4 %copy-start.3 = (s32[4,96,128]{2,1,0:T(8,128)S(1)}, s32[4,96,128]{2,1,0:T(8,128)}, u32[]{:S(2)}) copy-start(s32[4,96,128]{2,1,0:T(8,128)} %param.18) | copy-start | bytes 589828
  0.6 3.4 %copy-start.45 = (f32[4,96,128]{2,1,0:T(8,128)S(1)}, f32[4,96,128]{2,1,0:T(8,128)}, u32[]{:S(2)}) copy-start(f32[4,96,128]{2,1,0:T(8,128)} %param.17) | copy-start | bytes 589828
  1.8 52.6 %copy-start.5 = (f32[1,4,96,128]{3,2,1,0:T(8,128)}, f32[1,4,96,128]{3,2,1,0:T(8,128)S(1)}, u32[]{:S(2)}) copy-start(f32[1,4,96,128]{3,2,1,0:T(8,128)S(1)} %get-tuple-element.11) | copy-start | bytes 589828
  2.9 51.4 %copy-start.8 = (f32[1,4,96,128]{3,2,1,0:T(8,128)}, f32[1,4,96,128]{3,2,1,0:T(8,128)S(1)}, u32[]{:S(2)}) copy-start(f32[1,4,96,128]{3,2,1,0:T(8,128)S(1)} %get-tuple-element.9) | copy-start | bytes 589828
  6.4 69.1 %all-to-all-start = ((f32[64,5,4,128]{3,2,1,0:T(4,128)}), f32[64,5,4,128]{3,2,1,0:T(4,128)}, u32[]{:S(2)}, u32[]{:S(2)}) async-start(f32[64,5,4,128]{3,2,1,0:T(4,128)} %stack.49), calls=%async_computation | async-start | bytes 1310720 | tf_op jit(solution)/shard_map/all_to_all | solution.py:100
  26.9 47.8 %collective-permute-start.3 = (f32[5,4,1,128]{3,2,1,0:T(1,128)}, f32[5,4,1,128]{3,2,1,0:T(1,128)S(1)}, u32[]{:S(2)}, u32[]{:S(2)}) collective-permute-start(f32[5,4,1,128]{3,2,1,0:T(1,128)} %get-tuple-element.27), channel_id=1, source_target_pairs={{0,1},{1,2},{2,3},{3,4},{4,5},{5,6},{6,7},{8,9},{9,10},{10,11},{11... | collective-permute-start | bytes 30728 | tf_op jit(solution)/shard_map/ppermute | solution.py:19
  29.8 48.8 %collective-permute-start.2 = (f32[5,4,1,128]{3,1,0,2:T(4,128)}, f32[5,4,1,128]{3,1,0,2:T(4,128)}, u32[]{:S(2)}, u32[]{:S(2)}) collective-permute-start(f32[5,4,1,128]{3,1,0,2:T(4,128)} %bitcast.39), channel_id=1, source_target_pairs={{1,0},{2,1},{3,2},{4,3},{5,4},{6,5},{7,6},{9,8},{10,9},{11,10},{12... | collective-permute-start | bytes 30728 | tf_op jit(solution)/shard_map/ppermute | solution.py:20
  34.1 21.1 %copy-start.46 = (f32[3,96,128]{2,1,0:T(8,128)S(1)}, f32[3,96,128]{2,1,0:T(8,128)}, u32[]{:S(2)}) copy-start(f32[3,96,128]{2,1,0:T(8,128)} %param.24) | copy-start | bytes 442372
  36.2 36.4 %collective-permute-start = (f32[5,4,96,1]{2,1,3,0:T(4,128)}, f32[5,4,96,1]{2,1,3,0:T(4,128)}, u32[]{:S(2)}, u32[]{:S(2)}) collective-permute-start(f32[5,4,96,1]{2,1,3,0:T(4,128)} %copy.83), channel_id=1, source_target_pairs={{8,0},{16,8},{24,16},{32,24},{40,32},{48,40},{56,48},{64,56},{72,6... | collective-permute-start | bytes 23048 | tf_op jit(solution)/shard_map/ppermute | solution.py:20
  52.4 18.2 %collective-permute-start.1 = (f32[5,4,96,1]{2,1,3,0:T(4,128)S(1)}, f32[5,4,96,1]{2,1,3,0:T(4,128)}, u32[]{:S(2)}, u32[]{:S(2)}) collective-permute-start(f32[5,4,96,1]{2,1,3,0:T(4,128)S(1)} %copy.85), channel_id=1, source_target_pairs={{0,8},{8,16},{16,24},{24,32},{32,40},{40,48},{48,56},{56,64},{64,7... | collective-permute-start | bytes 23048 | tf_op jit(solution)/shard_map/ppermute | solution.py:19
  54.3 1.7 %copy-start.48 = (f32[96,128]{1,0:T(8,128)S(1)}, f32[96,128]{1,0:T(8,128)}, u32[]{:S(2)}) copy-start(f32[96,128]{1,0:T(8,128)} %param.21) | copy-start | bytes 147460
  54.4 1.7 %copy-start.49 = (f32[96,128]{1,0:T(8,128)S(1)}, f32[96,128]{1,0:T(8,128)}, u32[]{:S(2)}) copy-start(f32[96,128]{1,0:T(8,128)} %param.20) | copy-start | bytes 147460
  55.2 1.6 %copy-start.23 = (f32[3,96,128]{2,1,0:T(8,128)}, f32[3,96,128]{2,1,0:T(8,128)S(1)}, u32[]{:S(2)}) copy-start(f32[3,96,128]{2,1,0:T(8,128)S(1)} %fusion.99) | copy-start | bytes 442372
  55.2 1.7 %copy-start.47 = (f32[4]{0:T(128)S(1)}, f32[4]{0:T(128)}, u32[]{:S(2)}) copy-start(f32[4]{0:T(128)} %param.25) | copy-start | bytes 52
  79.5 1.5 copy-start.6
  79.5 1.5 copy-start.9
  79.5 1.6 %copy-start.21 = (f32[4,3,96,128]{3,2,1,0:T(8,128)S(1)}, f32[4,3,96,128]{3,2,1,0:T(8,128)}, u32[]{:S(2)}) copy-start(f32[4,3,96,128]{3,2,1,0:T(8,128)} %fusion.35) | copy-start | bytes 1769476
  79.5 1.6 %copy-start.25 = (f32[96,128]{1,0:T(8,128)S(1)}, f32[96,128]{1,0:T(8,128)}, u32[]{:S(2)}) copy-start(f32[96,128]{1,0:T(8,128)} %get-tuple-element.43) | copy-start | bytes 147460
  79.5 1.6 %copy-start.27 = (f32[96,128]{1,0:T(8,128)S(1)}, f32[96,128]{1,0:T(8,128)}, u32[]{:S(2)}) copy-start(f32[96,128]{1,0:T(8,128)} %get-tuple-element.40) | copy-start | bytes 147460
  79.5 1.6 %copy-start.39 = (f32[96,128]{1,0:T(8,128)S(1)}, f32[96,128]{1,0:T(8,128)}, u32[]{:S(2)}) copy-start(f32[96,128]{1,0:T(8,128)} %get-tuple-element.41) | copy-start | bytes 147460
  79.5 1.6 %copy-start.41 = (f32[96,128]{1,0:T(8,128)S(1)}, f32[96,128]{1,0:T(8,128)}, u32[]{:S(2)}) copy-start(f32[96,128]{1,0:T(8,128)} %get-tuple-element.42) | copy-start | bytes 147460
  79.5 1.6 %copy-start.43 = (f32[96,128]{1,0:T(8,128)S(1)}, f32[96,128]{1,0:T(8,128)}, u32[]{:S(2)}) copy-start(f32[96,128]{1,0:T(8,128)} %param.23) | copy-start | bytes 147460
  79.5 1.6 %copy-start.50 = (f32[4]{0:T(128)S(1)}, f32[4]{0:T(128)}, u32[]{:S(2)}) copy-start(f32[4]{0:T(128)} %mul.524) | copy-start | bytes 52
  86.9 55.0 %all-to-all-start.1 = ((f32[64,5,4,128]{3,2,1,0:T(4,128)}), f32[64,5,4,128]{3,2,1,0:T(4,128)}, u32[]{:S(2)}, u32[]{:S(2)}) async-start(f32[64,5,4,128]{3,2,1,0:T(4,128)} %stack.53), calls=%async_computation.1 | async-start | bytes 1310720 | tf_op jit(solution)/shard_map/all_to_all | solution.py:100
  92.4 47.6 %collective-permute-start.7 = (f32[5,4,1,128]{3,2,1,0:T(1,128)S(1)}, f32[5,4,1,128]{3,2,1,0:T(1,128)S(1)}, u32[]{:S(2)}, u32[]{:S(2)}) collective-permute-start(f32[5,4,1,128]{3,2,1,0:T(1,128)S(1)} %get-tuple-element.23), channel_id=1, source_target_pairs={{0,1},{1,2},{2,3},{3,4},{4,5},{5,6},{6,7},{8,9},{9,10},{10,11},{11... | collective-permute-start | bytes 30728 | tf_op jit(solution)/shard_map/ppermute | solution.py:19
  95.5 20.0 %copy-start.24 = (f32[3,96,128]{2,1,0:T(8,128)S(1)}, f32[3,96,128]{2,1,0:T(8,128)}, u32[]{:S(2)}) copy-start(f32[3,96,128]{2,1,0:T(8,128)} %copy-done.23) | copy-start | bytes 442372
  95.8 37.9 %collective-permute-start.5 = (f32[5,4,96,1]{2,1,3,0:T(4,128)S(1)}, f32[5,4,96,1]{2,1,3,0:T(4,128)S(1)}, u32[]{:S(2)}, u32[]{:S(2)}) collective-permute-start(f32[5,4,96,1]{2,1,3,0:T(4,128)S(1)} %copy.92), channel_id=1, source_target_pairs={{0,8},{8,16},{16,24},{24,32},{32,40},{40,48},{48,56},{56,64},{64,7... | collective-permute-start | bytes 23048 | tf_op jit(solution)/shard_map/ppermute | solution.py:19
  98.1 36.0 %collective-permute-start.4 = (f32[5,4,96,1]{2,1,3,0:T(4,128)S(1)}, f32[5,4,96,1]{2,1,3,0:T(4,128)}, u32[]{:S(2)}, u32[]{:S(2)}) collective-permute-start(f32[5,4,96,1]{2,1,3,0:T(4,128)S(1)} %copy.90), channel_id=1, source_target_pairs={{8,0},{16,8},{24,16},{32,24},{40,32},{48,40},{56,48},{64,56},{72,6... | collective-permute-start | bytes 23048 | tf_op jit(solution)/shard_map/ppermute | solution.py:20
  116.5 28.6 %collective-permute-start.6 = (f32[5,4,1,128]{3,2,1,0:T(1,128)}, f32[5,4,1,128]{3,2,1,0:T(1,128)}, u32[]{:S(2)}, u32[]{:S(2)}) collective-permute-start(f32[5,4,1,128]{3,2,1,0:T(1,128)} %get-tuple-element.22), channel_id=1, source_target_pairs={{1,0},{2,1},{3,2},{4,3},{5,4},{6,5},{7,6},{9,8},{10,9},{11,10},{12... | collective-permute-start | bytes 30728 | tf_op jit(solution)/shard_map/ppermute | solution.py:20
  141.1 4.8 %copy-start.4 = (s32[4,96,128]{2,1,0:T(8,128)S(1)}, s32[4,96,128]{2,1,0:T(8,128)}, u32[]{:S(2)}) copy-start(s32[4,96,128]{2,1,0:T(8,128)} %param.18) | copy-start | bytes 589828
  145.9 1.5 copy-start.7
  145.9 1.5 copy-start.10
  145.9 1.7 %copy-start.16 = (f32[5,4,97,128]{3,2,1,0:T(8,128)S(1)}, f32[5,4,97,128]{3,2,1,0:T(8,128)}, u32[]{:S(2)}) copy-start(f32[5,4,97,128]{3,2,1,0:T(8,128)} %maximum_maximum_fusion.1) | copy-start | bytes 2979844
  146.0 1.7 %copy-start.18 = (f32[1,4,96,128]{3,2,1,0:T(8,128)S(1)}, f32[1,4,96,128]{3,2,1,0:T(8,128)}, u32[]{:S(2)}) copy-start(f32[1,4,96,128]{3,2,1,0:T(8,128)} %copy-done.17) | copy-start | bytes 589828
  146.0 1.7 %copy-start.20 = (f32[1,4,96,128]{3,2,1,0:T(8,128)S(1)}, f32[1,4,96,128]{3,2,1,0:T(8,128)}, u32[]{:S(2)}) copy-start(f32[1,4,96,128]{3,2,1,0:T(8,128)} %copy-done.19) | copy-start | bytes 589828
  146.0 1.9 %copy-start.22 = (f32[4,3,96,128]{3,2,1,0:T(8,128)S(1)}, f32[4,3,96,128]{3,2,1,0:T(8,128)}, u32[]{:S(2)}) copy-start(f32[4,3,96,128]{3,2,1,0:T(8,128)} %fusion.34) | copy-start | bytes 1769476
  146.0 1.9 %copy-start.26 = (f32[96,128]{1,0:T(8,128)S(1)}, f32[96,128]{1,0:T(8,128)}, u32[]{:S(2)}) copy-start(f32[96,128]{1,0:T(8,128)} %get-tuple-element.43) | copy-start | bytes 147460
  146.0 1.9 %copy-start.28 = (f32[96,128]{1,0:T(8,128)S(1)}, f32[96,128]{1,0:T(8,128)}, u32[]{:S(2)}) copy-start(f32[96,128]{1,0:T(8,128)} %get-tuple-element.40) | copy-start | bytes 147460
  146.0 2.0 %copy-start.37 = (f32[4,96,128]{2,1,0:T(8,128)S(1)}, f32[4,96,128]{2,1,0:T(8,128)}, u32[]{:S(2)}) copy-start(f32[4,96,128]{2,1,0:T(8,128)} %get-tuple-element.32) | copy-start | bytes 589828
  146.0 2.0 %copy-start.38 = (f32[4,96,128]{2,1,0:T(8,128)S(1)}, f32[4,96,128]{2,1,0:T(8,128)}, u32[]{:S(2)}) copy-start(f32[4,96,128]{2,1,0:T(8,128)} %get-tuple-element.33) | copy-start | bytes 589828
  146.0 2.0 %copy-start.40 = (f32[96,128]{1,0:T(8,128)S(1)}, f32[96,128]{1,0:T(8,128)}, u32[]{:S(2)}) copy-start(f32[96,128]{1,0:T(8,128)} %get-tuple-element.41) | copy-start | bytes 147460
  146.0 2.0 %copy-start.42 = (f32[96,128]{1,0:T(8,128)S(1)}, f32[96,128]{1,0:T(8,128)}, u32[]{:S(2)}) copy-start(f32[96,128]{1,0:T(8,128)} %get-tuple-element.42) | copy-start | bytes 147460
  146.0 2.0 %copy-start.44 = (f32[96,128]{1,0:T(8,128)S(1)}, f32[96,128]{1,0:T(8,128)}, u32[]{:S(2)}) copy-start(f32[96,128]{1,0:T(8,128)} %param.23) | copy-start | bytes 147460
  146.1 2.0 %copy-start.51 = (f32[4]{0:T(128)S(1)}, f32[4]{0:T(128)}, u32[]{:S(2)}) copy-start(f32[4]{0:T(128)} %mul.524) | copy-start | bytes 52
  148.0 2.7 %copy-start.2 = (f32[5,4,96,1]{3,2,1,0:T(8,128)S(1)}, f32[5,4,96,1]{3,2,1,0:T(8,128)}, u32[]{:S(2)}) copy-start(f32[5,4,96,1]{3,2,1,0:T(8,128)} %copy.91) | copy-start | bytes 23044
  148.1 2.7 %copy-start.29 = (f32[1,4,96,128]{3,2,1,0:T(8,128)S(1)}, f32[1,4,96,128]{3,2,1,0:T(8,128)}, u32[]{:S(2)}) copy-start(f32[1,4,96,128]{3,2,1,0:T(8,128)} %reduce-window_subtract_fusion.2) | copy-start | bytes 589828
  148.1 2.7 %copy-start.32 = (s32[96,128]{1,0:T(8,128)S(1)}, s32[96,128]{1,0:T(8,128)}, u32[]{:S(2)}) copy-start(s32[96,128]{1,0:T(8,128)} %param.19) | copy-start | bytes 147460
  148.1 2.7 %copy-start.34 = (f32[96,128]{1,0:T(8,128)S(1)}, f32[96,128]{1,0:T(8,128)}, u32[]{:S(2)}) copy-start(f32[96,128]{1,0:T(8,128)} %param.22) | copy-start | bytes 147460
  (14 other events, 16.6 us)
